TPU v7x, 32 devices: a whole 2x2x4 slice. The times are simulated.
32 devices in a mesh: slab: 8 (over y, x, core), view: 4 (over z).
Axes of the slice: x: 2, y: 2, z: 4, core: 2. Of those that a mesh axis runs over, the one named last changes fastest.
Arguments:
- estimate: float32 [4, 1024, 1024], P(None, 'slab'), may hold values from 0.5 to 2
- views: float32 [4, 4, 1024, 1024], P('view', None, 'slab'), may hold values from 0.25 to 4
- psf: float32 [4, 1024, 1024], P('view', 'slab'), as said below
- pattern_mult: int32 [4, 8], P('view'), may hold values from 0 to 63
- pattern_shift: int32 [4, 8], P('view'), may hold values from 0 to 127
- interp: float32 [4, 8, 128], P('view'), may hold values from 0.05 to 0.45
Outputs:
- updated: float32 [4, 1024, 1024], P(None, 'slab')
Inputs may be any that keep to these rules, and one draw needn't show every extreme that they name: `psf`: every entry is positive.
All inputs are finite; a program needn't handle non-finite values.
Results may differ from a plain program's by a relative error of at most 0.0001.
Values sent between devices are 32-bit elements; how exact they have to be, the bound alone decides.
No kernel may reach another device: no remote copies, remote signals or barrier semaphores. Data moves between devices by JAX's collectives and lax.ppermute only.
A program may use at most 128 MiB of HBM per device.

v0:
```python
import math
import jax
import jax.numpy as jnp
from jax import lax
from jax.sharding import PartitionSpec as P

highest = lax.Precision.HIGHEST


def block_matrix(multiplier, shifting, weights):
    positions = jnp.arange(128, dtype=jnp.int32)
    first_col = ((2 * multiplier[:, None] + 1) * positions[None, :] + shifting[:, None]) % 128
    second_col = (first_col + 1) % 128
    columns = positions[None, None, :]
    lower = (columns == first_col[:, :, None]).astype(jnp.float32)
    upper = (columns == second_col[:, :, None]).astype(jnp.float32)
    return (1.0 - weights)[:, :, None] * lower + weights[:, :, None] * upper


def angle_tables(rows, cols, length):
    row_index = lax.iota(jnp.int32, rows)[:, None]
    col_index = lax.iota(jnp.int32, cols)[None, :]
    angles = (row_index * col_index % length).astype(jnp.float32) * (2.0 * math.pi / length)
    return (jnp.cos(angles), jnp.sin(angles))


def contract(form, real_part, imag_part, cosine, sine_table, direction, want_imag):
    real_cos = jnp.einsum(form, real_part, cosine, precision=highest)
    if imag_part is None:
        return (real_cos, direction * jnp.einsum(form, real_part, sine_table, precision=highest))
    imag_sin = jnp.einsum(form, imag_part, sine_table, precision=highest)
    out_real = real_cos - direction * imag_sin
    if not want_imag:
        return (out_real, None)
    real_sin = jnp.einsum(form, real_part, sine_table, precision=highest)
    imag_cos = jnp.einsum(form, imag_part, cosine, precision=highest)
    return (out_real, imag_cos + direction * real_sin)


def complex_times(real_part, imag_part, cosine, sine_table):
    return (
        real_part * cosine - imag_part * sine_table,
        real_part * sine_table + imag_part * cosine,
    )


def factored(real_part, imag_part, axis, direction, forward, want_imag):
    length = real_part.shape[axis]
    second = 128
    first = length // second
    if axis == 2:
        leading, trailing = ("rx", "")
    else:
        leading, trailing = ("r", "z")
    outer = real_part.shape
    shape = outer[:axis] + (first, second) + outer[axis + 1 :]
    real_part = real_part.reshape(shape)
    if imag_part is not None:
        imag_part = imag_part.reshape(shape)
    first_cos, first_sin = angle_tables(first, first, first)
    second_cos, second_sin = angle_tables(second, second, second)
    twist_cos, twist_sin = angle_tables(first, second, length)
    if axis == 1:
        twist_cos = twist_cos[:, :, None]
        twist_sin = twist_sin[:, :, None]
    twist_sin = direction * twist_sin
    if forward:
        real_part, imag_part = contract(
            leading + "ab" + trailing + ",ak->" + leading + "kb" + trailing,
            real_part,
            imag_part,
            first_cos,
            first_sin,
            direction,
            True,
        )
        real_part, imag_part = complex_times(real_part, imag_part, twist_cos, twist_sin)
        real_part, imag_part = contract(
            leading + "kb" + trailing + ",bm->" + leading + "km" + trailing,
            real_part,
            imag_part,
            second_cos,
            second_sin,
            direction,
            want_imag,
        )
    else:
        real_part, imag_part = contract(
            leading + "km" + trailing + ",mb->" + leading + "kb" + trailing,
            real_part,
            imag_part,
            second_cos,
            second_sin,
            direction,
            True,
        )
        real_part, imag_part = complex_times(real_part, imag_part, twist_cos, twist_sin)
        real_part, imag_part = contract(
            leading + "kb" + trailing + ",ka->" + leading + "ab" + trailing,
            real_part,
            imag_part,
            first_cos,
            first_sin,
            direction,
            want_imag,
        )
    real_part = real_part.reshape(outer)
    if imag_part is not None:
        imag_part = imag_part.reshape(outer)
    return (real_part, imag_part)


def to_columns(real_part, imag_part):
    depth_real, depth_imag = factored(real_part, imag_part, 2, -1.0, True, True)
    moved_real, moved_imag = (
        lax.all_to_all(depth_real, "slab", split_axis=2, concat_axis=1, tiled=True),
        lax.all_to_all(depth_imag, "slab", split_axis=2, concat_axis=1, tiled=True),
    )
    return factored(moved_real, moved_imag, 1, -1.0, True, True)


def to_planes(real_part, imag_part):
    width_real, width_imag = factored(real_part, imag_part, 1, 1.0, False, True)
    moved_real, moved_imag = (
        lax.all_to_all(width_real, "slab", split_axis=1, concat_axis=2, tiled=True),
        lax.all_to_all(width_imag, "slab", split_axis=1, concat_axis=2, tiled=True),
    )
    scaling = 1.0 / (width_real.shape[1] * moved_real.shape[2])
    out_real, out_imag = factored(moved_real, moved_imag, 2, 1.0, False, False)
    return (out_real * scaling, None)


def shards(estimate, views, psf, pattern_mult, pattern_shift, interp):
    row_count, slab_width, depth = estimate.shape
    blocks = block_matrix(pattern_mult[0], pattern_shift[0], interp[0])
    block_count = depth // 128
    shaped = estimate.reshape(row_count, slab_width, block_count, 128)
    sampled = jnp.einsum("bij,yxbj->yxbi", blocks, shaped, precision=highest).reshape(
        row_count, slab_width, depth
    )

    def pack(volume):
        return (volume, None)

    packed_real, packed_imag = pack(sampled)
    packed_real = jnp.concatenate([packed_real, psf], 0)
    spectra_real, spectra_imag = to_columns(packed_real, packed_imag)
    transfer_real = spectra_real[-1:]
    transfer_imag = spectra_imag[-1:]
    spectra_real = spectra_real[:-1]
    spectra_imag = spectra_imag[:-1]
    filtered_real = spectra_real * transfer_real - spectra_imag * transfer_imag
    filtered_imag = spectra_real * transfer_imag + spectra_imag * transfer_real
    blurred_real, blurred_imag = to_planes(filtered_real, filtered_imag)
    quotient = views[0] / blurred_real
    packed_real, packed_imag = pack(quotient)
    spectra_real, spectra_imag = to_columns(packed_real, packed_imag)
    filtered_real = spectra_real * transfer_real + spectra_imag * transfer_imag
    filtered_imag = spectra_imag * transfer_real - spectra_real * transfer_imag
    smeared_real, smeared_imag = to_planes(filtered_real, filtered_imag)
    correction = jnp.einsum(
        "bij,yxbi->yxbj",
        blocks,
        smeared_real.reshape(row_count, slab_width, block_count, 128),
        precision=highest,
    ).reshape(row_count, slab_width, depth)
    log_terms = jnp.log(correction)
    view_count = lax.axis_size("view")
    summed = lax.psum(log_terms, "view")
    return estimate * jnp.exp(summed / view_count)


def solution(mesh):
    placed = (
        P(None, "slab", None),
        P("view", None, "slab", None),
        P("view", "slab", None),
        P("view", None),
        P("view", None),
        P("view", None, None),
    )
    return jax.shard_map(
        shards, mesh=mesh, in_specs=placed, out_specs=P(None, "slab", None), check_vma=False
    )
```

profile of v0, /device:TPU:0, one launch (start us, length us, event | category | flops | bytes accessed | tf_op | source)
XLA Modules:
  0.0 555.8 jit_solution(18437681724977504398)
XLA Ops:
  20.8 4.7 subtract_bitcast_fusion.2
  35.7 5.2 all-to-all-start.1
  50.7 39.3 %all-to-all-done.1 = f32[5,128,1024]{1,0,2:T(8,128)} async-done(((f32[5,128,1024]{1,0,2:T(8,128)}), f32[5,128,1024]{1,0,2:T(8,128)}, u32[]{:S(2)}, u32[]{:S(2)}) %all-to-all-start.1) | async-done | bytes 2621472 | tf_op jit(solution)/shard_map/all_to_all | solution.py:117
  90.0 4.8 all-to-all-start
  98.1 3.8 fusion
  101.9 3.9 fusion.2
  105.8 37.9 %all-to-all-done = f32[5,128,1024]{1,0,2:T(8,128)} async-done(((f32[5,128,1024]{1,0,2:T(8,128)}), f32[5,128,1024]{1,0,2:T(8,128)}, u32[]{:S(2)}, u32[]{:S(2)}) %all-to-all-start) | async-done | bytes 2621472 | tf_op jit(solution)/shard_map/all_to_all | solution.py:116
  146.8 4.3 multiply_add_fusion
  185.9 4.4 all-to-all-start.2
  190.3 4.5 fusion.75
  200.9 16.1 %all-to-all-done.2 = f32[4,1024,128]{2,0,1:T(4,128)} async-done(((f32[4,1024,128]{2,0,1:T(4,128)}), f32[4,1024,128]{2,0,1:T(4,128)}, u32[]{:S(2)}, u32[]{:S(2)}) %all-to-all-start.2) | async-done | bytes 2097184 | tf_op jit(solution)/shard_map/all_to_all | solution.py:125
  217.0 4.5 all-to-all-start.3
  228.4 19.5 %all-to-all-done.3 = f32[4,1024,128]{2,0,1:T(4,128)} async-done(((f32[4,1024,128]{2,0,1:T(4,128)}), f32[4,1024,128]{2,0,1:T(4,128)}, u32[]{:S(2)}, u32[]{:S(2)}) %all-to-all-start.3) | async-done | bytes 2097184 | tf_op jit(solution)/shard_map/all_to_all | solution.py:126
  275.3 4.4 all-to-all-start.5
  279.6 4.0 fusion.69
  289.0 17.3 %all-to-all-done.5 = f32[4,128,1024]{1,0,2:T(4,128)} async-done(((f32[4,128,1024]{1,0,2:T(4,128)}), f32[4,128,1024]{1,0,2:T(4,128)}, u32[]{:S(2)}, u32[]{:S(2)}) %all-to-all-start.5) | async-done | bytes 2097184 | tf_op jit(solution)/shard_map/all_to_all | solution.py:117
  306.3 4.5 all-to-all-start.4
  319.5 17.8 %all-to-all-done.4 = f32[4,128,1024]{1,0,2:T(4,128)} async-done(((f32[4,128,1024]{1,0,2:T(4,128)}), f32[4,128,1024]{1,0,2:T(4,128)}, u32[]{:S(2)}, u32[]{:S(2)}) %all-to-all-start.4) | async-done | bytes 2097184 | tf_op jit(solution)/shard_map/all_to_all | solution.py:116
  375.3 4.4 all-to-all-start.6
  379.6 4.5 fusion.51
  390.2 16.1 %all-to-all-done.6 = f32[4,1024,128]{2,0,1:T(4,128)} async-done(((f32[4,1024,128]{2,0,1:T(4,128)}), f32[4,1024,128]{2,0,1:T(4,128)}, u32[]{:S(2)}, u32[]{:S(2)}) %all-to-all-start.6) | async-done | bytes 2097184 | tf_op jit(solution)/shard_map/all_to_all | solution.py:125
  406.3 4.3 all-to-all-start.7
  416.0 21.3 %all-to-all-done.7 = f32[4,1024,128]{2,0,1:T(4,128)} async-done(((f32[4,1024,128]{2,0,1:T(4,128)}), f32[4,1024,128]{2,0,1:T(4,128)}, u32[]{:S(2)}, u32[]{:S(2)}) %all-to-all-start.7) | async-done | bytes 2097184 | tf_op jit(solution)/shard_map/all_to_all | solution.py:126
  457.7 84.9 %all-reduce.2.cloned.1.call-done = f32[4,128,1024]{1,2,0:T(8,128)} async-done(((f32[4,128,1024]{1,2,0:T(8,128)}), f32[4,128,1024]{1,2,0:T(8,128)}) %all-reduce.2.cloned.1.call-update) | async-done | bytes 2097168 | tf_op jit(solution)/shard_map/psum | solution.py:169
  (116 shorter events, 205.1 us)
Async XLA Ops:
  18.4 2.4 copy-start
  25.5 3.1 copy-start.1
  35.7 54.4 %all-to-all-start.1 = ((f32[5,128,1024]{1,0,2:T(8,128)}), f32[5,128,1024]{1,0,2:T(8,128)}, u32[]{:S(2)}, u32[]{:S(2)}) async-start(f32[5,128,1024]{1,0,2:T(8,128)} %copy.157), calls=%async_computation.1 | async-start | bytes 8388608 | tf_op jit(solution)/shard_map/all_to_all | solution.py:117
  40.8 3.0 copy-start.2
  90.0 53.7 %all-to-all-start = ((f32[5,128,1024]{1,0,2:T(8,128)}), f32[5,128,1024]{1,0,2:T(8,128)}, u32[]{:S(2)}, u32[]{:S(2)}) async-start(f32[5,128,1024]{1,0,2:T(8,128)} %copy.151), calls=%async_computation | async-start | bytes 8388608 | tf_op jit(solution)/shard_map/all_to_all | solution.py:116
  146.8 4.3 copy-start.6
  176.7 3.3 copy-start.4
  185.9 31.0 %all-to-all-start.2 = ((f32[4,1024,128]{2,0,1:T(4,128)}), f32[4,1024,128]{2,0,1:T(4,128)}, u32[]{:S(2)}, u32[]{:S(2)}) async-start(f32[4,1024,128]{2,0,1:T(4,128)} %copy.176), calls=%async_computation.2 | async-start | bytes 4194304 | tf_op jit(solution)/shard_map/all_to_all | solution.py:125
  200.9 20.6 %copy-start.10 = (f32[1,4,128,1024]{3,2,1,0:T(8,128)S(1)}, f32[1,4,128,1024]{3,2,1,0:T(8,128)}, u32[]{:S(2)}) copy-start(f32[1,4,128,1024]{3,2,1,0:T(8,128)} %param.7) | copy-start | bytes 6291460
  217.0 31.0 %all-to-all-start.3 = ((f32[4,1024,128]{2,0,1:T(4,128)}), f32[4,1024,128]{2,0,1:T(4,128)}, u32[]{:S(2)}, u32[]{:S(2)}) async-start(f32[4,1024,128]{2,0,1:T(4,128)} %copy.181), calls=%async_computation.3 | async-start | bytes 4194304 | tf_op jit(solution)/shard_map/all_to_all | solution.py:126
  249.7 2.1 copy-start.7
  256.5 3.1 copy-start.11
  267.1 2.5 copy-start.5
  275.3 31.0 %all-to-all-start.5 = ((f32[4,128,1024]{1,0,2:T(4,128)}), f32[4,128,1024]{1,0,2:T(4,128)}, u32[]{:S(2)}, u32[]{:S(2)}) async-start(f32[4,128,1024]{1,0,2:T(4,128)} %copy.195), calls=%async_computation.5 | async-start | bytes 4194304 | tf_op jit(solution)/shard_map/all_to_all | solution.py:117
  306.3 31.0 %all-to-all-start.4 = ((f32[4,128,1024]{1,0,2:T(4,128)}), f32[4,128,1024]{1,0,2:T(4,128)}, u32[]{:S(2)}, u32[]{:S(2)}) async-start(f32[4,128,1024]{1,0,2:T(4,128)} %copy.189), calls=%async_computation.4 | async-start | bytes 4194304 | tf_op jit(solution)/shard_map/all_to_all | solution.py:116
  339.6 3.7 copy-start.9
  366.2 2.9 copy-start.3
  375.3 31.0 %all-to-all-start.6 = ((f32[4,1024,128]{2,0,1:T(4,128)}), f32[4,1024,128]{2,0,1:T(4,128)}, u32[]{:S(2)}, u32[]{:S(2)}) async-start(f32[4,1024,128]{2,0,1:T(4,128)} %copy.214), calls=%async_computation.6 | async-start | bytes 4194304 | tf_op jit(solution)/shard_map/all_to_all | solution.py:125
  406.3 31.0 %all-to-all-start.7 = ((f32[4,1024,128]{2,0,1:T(4,128)}), f32[4,1024,128]{2,0,1:T(4,128)}, u32[]{:S(2)}, u32[]{:S(2)}) async-start(f32[4,1024,128]{2,0,1:T(4,128)} %copy.219), calls=%async_computation.7 | async-start | bytes 4194304 | tf_op jit(solution)/shard_map/all_to_all | solution.py:126
  410.6 132.0 %all-reduce.2.cloned.1.call-start = ((), (), s32[]{:S(2)}) async-start(), calls=%async_computation.8 | async-start | bytes 4194304 | tf_op jit(solution)/shard_map/psum | solution.py:169
  439.0 2.1 copy-start.8
  448.7 3.3 copy-start.12
Sparse Core Ops, SparseCore 0:
  455.9 86.6 all-reduce.1
where the time goes:
time: 560 us; the launch traced here: 556 us
  waiting for transfers between devices  270 us (48%)
  matrix products  172 us (31%)
  local copies, waits for them, and re-layouts  55.7 us (10%)
  starting transfers between devices  36.6 us (7%)
  between operations  14.4 us (3%)
  other arithmetic  7.07 us (1%)
    psum x1, waiting for transfers between devices, shards(): summed = lax.psum(log_terms, 'view')  84.9 us
    all_to_all x2, waiting for transfers between devices, to_columns(): lax.all_to_all(depth_imag, 'slab', split_axis=2, concat_axis=1, tiled=True)  56.6 us
    all_to_all x2, waiting for transfers between devices, to_columns(): lax.all_to_all(depth_real, 'slab', split_axis=2, concat_axis=1, tiled=True)  55.7 us
    dot_general x16, matrix products, contract(): real_cos = jnp.einsum(form, real_part, cosine, precision=highest)  48.2 us
    dot_general x14, matrix products, contract(): imag_sin = jnp.einsum(form, imag_part, sine_table, precision=highest)  41.1 us
    all_to_all x2, waiting for transfers between devices, to_planes(): lax.all_to_all(width_imag, 'slab', split_axis=1, concat_axis=2, tiled=True)  40.8 us
    dot_general x12, matrix products, contract(): real_sin = jnp.einsum(form, real_part, sine_table, precision=highest)  36.4 us
    dot_general x12, matrix products, contract(): imag_cos = jnp.einsum(form, imag_part, cosine, precision=highest)  35.7 us
  transfers between devices with their start and end apart: 9, of which 9 were waited for; matrix products, arithmetic and copies ran while one was open for 13% of the time, Pallas kernels for 0%

commit v1 on v0

--- a/solution.py
+++ b/solution.py
@@ -5,6 +5,22 @@
 from jax.sharding import PartitionSpec as P
 
 highest = lax.Precision.HIGHEST
+
+
+def swapped_with_each(value, axis, split, join):
+    ways, here = (lax.axis_size(axis), lax.axis_index(axis))
+    width = value.shape[split] // ways
+    dims = list(value.shape)
+    dims[split] = width
+    height = dims[join]
+    dims[join] = height * ways
+    full = jnp.zeros(dims, value.dtype)
+    for mask in range(ways):
+        part = lax.dynamic_slice_in_dim(value, (here ^ mask) * width, width, axis=split)
+        if mask:
+            part = lax.ppermute(part, axis, [(d, d ^ mask) for d in range(ways)])
+        full = lax.dynamic_update_slice_in_dim(full, part, (here ^ mask) * height, axis=join)
+    return full
 
 
 def block_matrix(multiplier, shifting, weights):
@@ -113,7 +129,7 @@
 def to_columns(real_part, imag_part):
     depth_real, depth_imag = factored(real_part, imag_part, 2, -1.0, True, True)
     moved_real, moved_imag = (
-        lax.all_to_all(depth_real, "slab", split_axis=2, concat_axis=1, tiled=True),
+        swapped_with_each(depth_real, "slab", 2, 1),
         lax.all_to_all(depth_imag, "slab", split_axis=2, concat_axis=1, tiled=True),
     )
     return factored(moved_real, moved_imag, 1, -1.0, True, True)

time: 560 us -> 542 us (0.968)
  waiting for transfers between devices: 270 us -> 230 us
  local copies, waits for them, and re-layouts: 55.7 us -> 72.2 us
    ppermute x0 -> x14, waiting for transfers between devices: none -> 72 us  [swapped_with_each(): part = lax.ppermute(part, axis, [(d, d ^ mask) for d in range(ways)])]
    all_to_all x2, waiting for transfers between devices: 56.6 us -> 0.01 us  [to_columns(): lax.all_to_all(depth_imag, 'slab', split_axis=2, concat_axis=1, tiled=True)]
    all_to_all x2 -> x0, waiting for transfers between devices: 55.7 us -> none  [to_columns(): lax.all_to_all(depth_real, 'slab', split_axis=2, concat_axis=1, tiled=True)]
    dynamic_update_slice x0 -> x16, local copies, waits for them, and re-layouts: none -> 15 us  [swapped_with_each(): lax.dynamic_update_slice_in_dim(full, part, (here ^ mask) * height, axis=...]
    ppermute x0 -> x14, starting transfers between devices: none -> 13.2 us  [swapped_with_each(): part = lax.ppermute(part, axis, [(d, d ^ mask) for d in range(ways)])]
    unnamed x29 -> x49, local copies, waits for them, and re-layouts: 5.07 us -> 14.7 us
    all_to_all x2 -> x0, starting transfers between devices: 9.29 us -> none  [to_columns(): lax.all_to_all(depth_real, 'slab', split_axis=2, concat_axis=1, tiled=True)]
    reshape x4 -> x2, local copies, waits for them, and re-layouts: 11.8 us -> 5.34 us  [factored(): real_part = real_part.reshape(outer)]
  transfers between devices with their start and end apart: 9 -> 21, of which waited for: 9 -> 13; matrix products, arithmetic and copies ran while one was open for 13% -> 14% of each run, Pallas kernels for 0% -> 0%
where the time goes in v1:
time: 542 us; the launch traced here: 538 us
  waiting for transfers between devices  230 us (42%)
  matrix products  173 us (32%)
  local copies, waits for them, and re-layouts  72.2 us (13%)
  starting transfers between devices  40.9 us (8%)
  between operations  14.5 us (3%)
  other arithmetic  7.1 us (1%)
    psum x1, waiting for transfers between devices, shards(): summed = lax.psum(log_terms, 'view')  85.1 us
    ppermute x14, waiting for transfers between devices, swapped_with_each(): part = lax.ppermute(part, axis, [(d, d ^ mask) for d in range(ways)])  72 us
    dot_general x16, matrix products, contract(): real_cos = jnp.einsum(form, real_part, cosine, precision=highest)  51.1 us
    all_to_all x2, waiting for transfers between devices, to_planes(): lax.all_to_all(width_imag, 'slab', split_axis=1, concat_axis=2, tiled=True)  40.6 us
    dot_general x14, matrix products, contract(): imag_sin = jnp.einsum(form, imag_part, sine_table, precision=highest)  39.1 us
    dot_general x12, matrix products, contract(): real_sin = jnp.einsum(form, real_part, sine_table, precision=highest)  38.8 us
    dot_general x12, matrix products, contract(): imag_cos = jnp.einsum(form, imag_part, cosine, precision=highest)  33.6 us
    all_to_all x2, waiting for transfers between devices, to_planes(): lax.all_to_all(width_real, 'slab', split_axis=1, concat_axis=2, tiled=True)  32.2 us
  transfers between devices with their start and end apart: 21, of which 13 were waited for; matrix products, arithmetic and copies ran while one was open for 14% of the time, Pallas kernels for 0%

profile of v1, /device:TPU:0, one launch (start us, length us, event | category | flops | bytes accessed | tf_op | source)
XLA Modules:
  0.0 537.6 jit_solution(6099191033845274265)
XLA Ops:
  20.5 4.7 subtract_bitcast_fusion.2
  35.4 5.2 all-to-all-start
  59.8 36.8 %collective-permute-done.1 = f32[5,128,128]{2,1,0:T(8,128)} collective-permute-done((f32[5,128,128]{2,1,0:T(8,128)S(1)}, f32[5,128,128]{2,1,0:T(8,128)}, u32[]{:S(2)}, u32[]{:S(2)}) %collective-permute-start.1) | collective-permute-done | bytes 327712 | tf_op jit(solution)/shard_map/ppermute | solution.py:21
  98.4 3.9 collective-permute-done.2
  106.5 5.0 collective-permute-done.5
  112.3 4.7 collective-permute-done.6
  126.0 5.5 %multiply_subtract_fusion = f32[8,5,128,128]{3,0,2,1:T(8,128)S(1)} fusion(f32[8,5,128,128]{3,0,2,1:T(8,128)S(1)} %fusion.2, f32[5,8,128,128]{3,2,1,0:T(8,128)} %bitcast.20), kind=kOutput, calls=%fused_computation.10 | convolution fusion | flops 64226176 | bytes 7864320 | tf_op jit(solution)/shard_map/rabz,ak->rkbz/dot_general | solution.py:44
  131.6 6.3 %subtract_bitcast_fusion.1 = (f32[5,8,128,128]{3,1,2,0:T(8,128)S(1)}, f32[5,8,128,128]{3,1,2,0:T(8,128)S(1)}) fusion(f32[8,5,128,128]{3,0,2,1:T(8,128)S(1)} %multiply_subtract_fusion, f32[8,128]{0,1:T(8,128)S(1)} %copy.184, f32[8,128]{0,1:T(8,128)S(1)} %copy.182, f32[8,5,128,128]{3,0,2,1:T(8,128)S(1)} %fusion, f32[5,8,128,128]{3,2,1,0:T(8,128)} %bitcast.20), kind=kOutput, calls=%fused_computation.8 | convolution fusion | flops 68158336 | bytes 13115392 | tf_op jit(solution)/shard_map/rabz,ak->rkbz/dot_general | solution.py:51
  169.3 4.3 all-to-all-start.1
  173.6 4.5 fusion.75
  184.2 16.1 %all-to-all-done.1 = f32[4,1024,128]{2,0,1:T(4,128)} async-done(((f32[4,1024,128]{2,0,1:T(4,128)}), f32[4,1024,128]{2,0,1:T(4,128)}, u32[]{:S(2)}, u32[]{:S(2)}) %all-to-all-start.1) | async-done | bytes 2097184 | tf_op jit(solution)/shard_map/all_to_all | solution.py:141
  200.3 4.8 all-to-all-start.2
  212.0 19.3 %all-to-all-done.2 = f32[4,1024,128]{2,0,1:T(4,128)} async-done(((f32[4,1024,128]{2,0,1:T(4,128)}), f32[4,1024,128]{2,0,1:T(4,128)}, u32[]{:S(2)}, u32[]{:S(2)}) %all-to-all-start.2) | async-done | bytes 2097184 | tf_op jit(solution)/shard_map/all_to_all | solution.py:142
  258.6 4.3 all-to-all-start.3
  262.9 4.0 fusion.69
  285.8 9.0 %collective-permute-done.8 = f32[4,128,128]{2,1,0:T(8,128)} collective-permute-done((f32[4,128,128]{2,1,0:T(8,128)}, f32[4,128,128]{2,1,0:T(8,128)}, u32[]{:S(2)}, u32[]{:S(2)}) %collective-permute-start.8) | collective-permute-done | bytes 262176 | tf_op jit(solution)/shard_map/ppermute | solution.py:21
  302.4 4.4 collective-permute-done.12
  306.9 4.6 collective-permute-done.13
  356.6 4.5 all-to-all-start.4
  361.1 4.5 fusion.47
  371.7 16.1 %all-to-all-done.4 = f32[4,1024,128]{2,0,1:T(4,128)} async-done(((f32[4,1024,128]{2,0,1:T(4,128)}), f32[4,1024,128]{2,0,1:T(4,128)}, u32[]{:S(2)}, u32[]{:S(2)}) %all-to-all-start.4) | async-done | bytes 2097184 | tf_op jit(solution)/shard_map/all_to_all | solution.py:141
  387.8 4.4 all-to-all-start.5
  397.5 21.3 %all-to-all-done.5 = f32[4,1024,128]{2,0,1:T(4,128)} async-done(((f32[4,1024,128]{2,0,1:T(4,128)}), f32[4,1024,128]{2,0,1:T(4,128)}, u32[]{:S(2)}, u32[]{:S(2)}) %all-to-all-start.5) | async-done | bytes 2097184 | tf_op jit(solution)/shard_map/all_to_all | solution.py:142
  439.2 85.1 %all-reduce.2.cloned.1.call-done = f32[4,128,1024]{1,2,0:T(8,128)} async-done(((f32[4,128,1024]{1,2,0:T(8,128)}), f32[4,128,1024]{1,2,0:T(8,128)}) %all-reduce.2.cloned.1.call-update) | async-done | bytes 2097168 | tf_op jit(solution)/shard_map/psum | solution.py:185
  (176 shorter events, 239.4 us)
Async XLA Ops:
  10.0 3.7 copy-start.13
  35.4 82.5 %all-to-all-start = ((f32[5,128,1024]{1,0,2:T(8,128)}), f32[5,128,1024]{1,0,2:T(8,128)}, u32[]{:S(2)}, u32[]{:S(2)}) async-start(f32[5,128,1024]{1,0,2:T(8,128)} %copy.180), calls=%async_computation | async-start | bytes 8388608 | tf_op jit(solution)/shard_map/all_to_all | solution.py:133
  47.2 8.3 %collective-permute-start = (f32[5,128,128]{2,1,0:T(8,128)S(1)}, f32[5,128,128]{2,1,0:T(8,128)}, u32[]{:S(2)}, u32[]{:S(2)}) collective-permute-start(f32[5,128,128]{2,1,0:T(8,128)S(1)} %copy.318), channel_id=1, source_target_pairs={{0,4},{4,0},{8,12},{12,8},{16,20},{20,16},{24,28},{28,24},{1,5},{5... | collective-permute-start | bytes 983048 | tf_op jit(solution)/shard_map/ppermute | solution.py:21
  47.9 48.7 %collective-permute-start.1 = (f32[5,128,128]{2,1,0:T(8,128)S(1)}, f32[5,128,128]{2,1,0:T(8,128)}, u32[]{:S(2)}, u32[]{:S(2)}) collective-permute-start(f32[5,128,128]{2,1,0:T(8,128)S(1)} %copy.319), channel_id=1, source_target_pairs={{0,8},{4,12},{8,0},{12,4},{16,24},{20,28},{24,16},{28,20},{1,9},{5... | collective-permute-start | bytes 983048 | tf_op jit(solution)/shard_map/ppermute | solution.py:21
  50.0 52.2 %collective-permute-start.2 = (f32[5,128,128]{2,1,0:T(8,128)S(1)}, f32[5,128,128]{2,1,0:T(8,128)}, u32[]{:S(2)}, u32[]{:S(2)}) collective-permute-start(f32[5,128,128]{2,1,0:T(8,128)S(1)} %copy.320), channel_id=1, source_target_pairs={{0,12},{4,8},{8,4},{12,0},{16,28},{20,24},{24,20},{28,16},{1,13},{... | collective-permute-start | bytes 983048 | tf_op jit(solution)/shard_map/ppermute | solution.py:21
  50.3 53.6 %collective-permute-start.3 = (f32[5,128,128]{2,1,0:T(8,128)S(1)}, f32[5,128,128]{2,1,0:T(8,128)}, u32[]{:S(2)}, u32[]{:S(2)}) collective-permute-start(f32[5,128,128]{2,1,0:T(8,128)S(1)} %copy.321), channel_id=1, source_target_pairs={{0,16},{4,20},{8,24},{12,28},{16,0},{20,4},{24,8},{28,12},{1,17},{... | collective-permute-start | bytes 983048 | tf_op jit(solution)/shard_map/ppermute | solution.py:21
  52.3 53.4 %collective-permute-start.4 = (f32[5,128,128]{2,1,0:T(8,128)S(1)}, f32[5,128,128]{2,1,0:T(8,128)S(1)}, u32[]{:S(2)}, u32[]{:S(2)}) collective-permute-start(f32[5,128,128]{2,1,0:T(8,128)S(1)} %copy.322), channel_id=1, source_target_pairs={{0,20},{4,16},{8,28},{12,24},{16,4},{20,0},{24,12},{28,8},{1,21},{... | collective-permute-start | bytes 983048 | tf_op jit(solution)/shard_map/ppermute | solution.py:21
  55.5 56.0 %collective-permute-start.5 = (f32[5,128,128]{2,1,0:T(8,128)S(1)}, f32[5,128,128]{2,1,0:T(8,128)S(1)}, u32[]{:S(2)}, u32[]{:S(2)}) collective-permute-start(f32[5,128,128]{2,1,0:T(8,128)S(1)} %copy.323), channel_id=1, source_target_pairs={{0,24},{4,28},{8,16},{12,20},{16,8},{20,12},{24,0},{28,4},{1,25},{... | collective-permute-start | bytes 983048 | tf_op jit(solution)/shard_map/ppermute | solution.py:21
  96.6 20.4 %collective-permute-start.6 = (f32[5,128,128]{2,1,0:T(8,128)S(1)}, f32[5,128,128]{2,1,0:T(8,128)S(1)}, u32[]{:S(2)}, u32[]{:S(2)}) collective-permute-start(f32[5,128,128]{2,1,0:T(8,128)S(1)} %copy.324), channel_id=1, source_target_pairs={{0,28},{4,24},{8,20},{12,16},{16,12},{20,8},{24,4},{28,0},{1,29},{... | collective-permute-start | bytes 983048 | tf_op jit(solution)/shard_map/ppermute | solution.py:21
  169.3 31.0 %all-to-all-start.1 = ((f32[4,1024,128]{2,0,1:T(4,128)}), f32[4,1024,128]{2,0,1:T(4,128)}, u32[]{:S(2)}, u32[]{:S(2)}) async-start(f32[4,1024,128]{2,0,1:T(4,128)} %copy.200), calls=%async_computation.1 | async-start | bytes 4194304 | tf_op jit(solution)/shard_map/all_to_all | solution.py:141
  184.2 20.9 %copy-start.9 = (f32[1,4,128,1024]{3,2,1,0:T(8,128)S(1)}, f32[1,4,128,1024]{3,2,1,0:T(8,128)}, u32[]{:S(2)}) copy-start(f32[1,4,128,1024]{3,2,1,0:T(8,128)} %param.7) | copy-start | bytes 6291460
  200.3 31.0 %all-to-all-start.2 = ((f32[4,1024,128]{2,0,1:T(4,128)}), f32[4,1024,128]{2,0,1:T(4,128)}, u32[]{:S(2)}, u32[]{:S(2)}) async-start(f32[4,1024,128]{2,0,1:T(4,128)} %copy.205), calls=%async_computation.2 | async-start | bytes 4194304 | tf_op jit(solution)/shard_map/all_to_all | solution.py:142
  258.6 53.0 %all-to-all-start.3 = ((f32[4,128,1024]{1,0,2:T(4,128)}), f32[4,128,1024]{1,0,2:T(4,128)}, u32[]{:S(2)}, u32[]{:S(2)}) async-start(f32[4,128,1024]{1,0,2:T(4,128)} %copy.226), calls=%async_computation.3 | async-start | bytes 4194304 | tf_op jit(solution)/shard_map/all_to_all | solution.py:133
  271.3 11.6 %collective-permute-start.7 = (f32[4,128,128]{2,1,0:T(8,128)}, f32[4,128,128]{2,1,0:T(8,128)}, u32[]{:S(2)}, u32[]{:S(2)}) collective-permute-start(f32[4,128,128]{2,1,0:T(8,128)} %copy.326), channel_id=1, source_target_pairs={{0,4},{4,0},{8,12},{12,8},{16,20},{20,16},{24,28},{28,24},{1,5},{5... | collective-permute-start | bytes 786440 | tf_op jit(solution)/shard_map/ppermute | solution.py:21
  272.5 22.2 %collective-permute-start.8 = (f32[4,128,128]{2,1,0:T(8,128)}, f32[4,128,128]{2,1,0:T(8,128)}, u32[]{:S(2)}, u32[]{:S(2)}) collective-permute-start(f32[4,128,128]{2,1,0:T(8,128)} %copy.327), channel_id=1, source_target_pairs={{0,8},{4,12},{8,0},{12,4},{16,24},{20,28},{24,16},{28,20},{1,9},{5... | collective-permute-start | bytes 786440 | tf_op jit(solution)/shard_map/ppermute | solution.py:21
  275.9 23.6 %collective-permute-start.9 = (f32[4,128,128]{2,1,0:T(8,128)}, f32[4,128,128]{2,1,0:T(8,128)}, u32[]{:S(2)}, u32[]{:S(2)}) collective-permute-start(f32[4,128,128]{2,1,0:T(8,128)} %copy.328), channel_id=1, source_target_pairs={{0,12},{4,8},{8,4},{12,0},{16,28},{20,24},{24,20},{28,16},{1,13},{... | collective-permute-start | bytes 786440 | tf_op jit(solution)/shard_map/ppermute | solution.py:21
  276.8 23.7 %collective-permute-start.10 = (f32[4,128,128]{2,1,0:T(8,128)}, f32[4,128,128]{2,1,0:T(8,128)}, u32[]{:S(2)}, u32[]{:S(2)}) collective-permute-start(f32[4,128,128]{2,1,0:T(8,128)} %copy.329), channel_id=1, source_target_pairs={{0,16},{4,20},{8,24},{12,28},{16,0},{20,4},{24,8},{28,12},{1,17},{... | collective-permute-start | bytes 786440 | tf_op jit(solution)/shard_map/ppermute | solution.py:21
  279.3 22.1 %collective-permute-start.11 = (f32[4,128,128]{2,1,0:T(8,128)}, f32[4,128,128]{2,1,0:T(8,128)}, u32[]{:S(2)}, u32[]{:S(2)}) collective-permute-start(f32[4,128,128]{2,1,0:T(8,128)} %copy.330), channel_id=1, source_target_pairs={{0,20},{4,16},{8,28},{12,24},{16,4},{20,0},{24,12},{28,8},{1,21},{... | collective-permute-start | bytes 786440 | tf_op jit(solution)/shard_map/ppermute | solution.py:21
  282.9 23.9 %collective-permute-start.12 = (f32[4,128,128]{2,1,0:T(8,128)}, f32[4,128,128]{2,1,0:T(8,128)S(1)}, u32[]{:S(2)}, u32[]{:S(2)}) collective-permute-start(f32[4,128,128]{2,1,0:T(8,128)} %copy.331), channel_id=1, source_target_pairs={{0,24},{4,28},{8,16},{12,20},{16,8},{20,12},{24,0},{28,4},{1,25},{... | collective-permute-start | bytes 786440 | tf_op jit(solution)/shard_map/ppermute | solution.py:21
  294.8 16.7 %collective-permute-start.13 = (f32[4,128,128]{2,1,0:T(8,128)}, f32[4,128,128]{2,1,0:T(8,128)S(1)}, u32[]{:S(2)}, u32[]{:S(2)}) collective-permute-start(f32[4,128,128]{2,1,0:T(8,128)} %copy.332), channel_id=1, source_target_pairs={{0,28},{4,24},{8,20},{12,16},{16,12},{20,8},{24,4},{28,0},{1,29},{... | collective-permute-start | bytes 786440 | tf_op jit(solution)/shard_map/ppermute | solution.py:21
  315.1 3.6 copy-start.3
  356.6 31.2 %all-to-all-start.4 = ((f32[4,1024,128]{2,0,1:T(4,128)}), f32[4,1024,128]{2,0,1:T(4,128)}, u32[]{:S(2)}, u32[]{:S(2)}) async-start(f32[4,1024,128]{2,0,1:T(4,128)} %copy.246), calls=%async_computation.4 | async-start | bytes 4194304 | tf_op jit(solution)/shard_map/all_to_all | solution.py:141
  387.8 31.0 %all-to-all-start.5 = ((f32[4,1024,128]{2,0,1:T(4,128)}), f32[4,1024,128]{2,0,1:T(4,128)}, u32[]{:S(2)}, u32[]{:S(2)}) async-start(f32[4,1024,128]{2,0,1:T(4,128)} %copy.251), calls=%async_computation.5 | async-start | bytes 4194304 | tf_op jit(solution)/shard_map/all_to_all | solution.py:142
  392.2 132.2 %all-reduce.2.cloned.1.call-start = ((), (), s32[]{:S(2)}) async-start(), calls=%async_computation.6 | async-start | bytes 4194304 | tf_op jit(solution)/shard_map/psum | solution.py:185
  (12 other events, 31.9 us)
Sparse Core Ops, SparseCore 0:
  437.4 86.8 all-reduce.1
